TPU v7x, 256 devices: a whole 4x4x8 slice. The times are simulated.
256 devices in a mesh: dp: 16 (over y_lo, x, core), tensor: 16 (over z, y_hi).
Axes of the slice: x: 4, y: 4 (y_hi: 2, y_lo: 2; y = y_hi * 2 + y_lo), z: 8, core: 2. Of those that a mesh axis runs over, the one named last changes fastest.
Arguments:
- gate_pre: bfloat16 [8192, 14336], P('dp', 'tensor'), may hold values from -6 to 6
- up_pre: bfloat16 [8192, 14336], P('dp', 'tensor'), may hold values from -6 to 6
- grad_out: bfloat16 [8192, 4096], P(('dp', 'tensor')), may hold values from -24 to 24
- codes: bfloat16 [14336, 4096], P('tensor'), as said below
- scales: int32 [448, 4096], P('tensor'), may hold values from 117 to 120
Outputs:
- out: bfloat16 [8192, 4096], P(('dp', 'tensor'))
- grad_gate: bfloat16 [8192, 14336], P('dp', 'tensor')
- grad_up: bfloat16 [8192, 14336], P('dp', 'tensor')
- grad_weight: bfloat16 [14336, 4096], P('tensor', 'dp')
Inputs may be any that keep to these rules, and one draw needn't show every extreme that they name: `codes`: every entry is an FP8 E4M3 normal value (sign, exponent field 4 to 9, three mantissa bits), held exactly.
All inputs are finite; a program needn't handle non-finite values.
Results may differ from a plain program's by a relative error of at most 0.022.
Values may be sent and summed in bfloat16 or wider, within the bound.
No kernel may reach another device: no remote copies, remote signals or barrier semaphores. Data moves between devices by JAX's collectives and lax.ppermute only.
A program may use at most 128 MiB of HBM per device.

v0:
```python
import jax
import jax.numpy as jnp
from jax import lax
from jax.experimental.layout import Layout, with_layout_constraint
from jax.sharding import Mesh, PartitionSpec as P

DP = ("dy", "dx", "dc")
TP = ("tz", "ty")


def decode(codes, scales):
    factor = jnp.exp2(scales.astype(jnp.float32) - 127.0).astype(jnp.bfloat16)
    blocks = codes.reshape(scales.shape[0], 32, codes.shape[1]) * factor[:, None, :]
    return blocks.reshape(codes.shape)


def exchange(value, axis, size, shift):
    perm = [(i, (i + shift) % size) for i in range(size)]
    return lax.ppermute(value, axis, perm)


def weight_gradient(hidden, cotangent):
    n_x = cotangent.shape[1] // 1024
    width = 256
    partial = lax.dot_general(
        cotangent, hidden, (((0,), (0,)), ((), ())), preferred_element_type=jnp.float32
    ).astype(jnp.bfloat16)
    partial = with_layout_constraint(partial, Layout(major_to_minor=(0, 1)))
    parts = partial.reshape(2, n_x, 2, width, partial.shape[1])
    dc = lax.axis_index("dc")
    mine = jnp.take(parts, dc, axis=2)
    arrived = exchange(jnp.take(parts, 1 - dc, axis=2), "dc", 2, 1)
    total = mine.astype(jnp.float32) + arrived.astype(jnp.float32)
    total = with_layout_constraint(total, Layout(major_to_minor=(0, 1, 2, 3)))
    sent = total.astype(jnp.bfloat16)
    dx = lax.axis_index("dx")
    acc = jnp.take(total, dx, axis=1)
    for shift in range(1, n_x):
        block = jnp.take(sent, (dx + shift) % n_x, axis=1)
        acc = acc + exchange(block, "dx", n_x, shift).astype(jnp.float32)
    dy = lax.axis_index("dy")
    sent = acc.astype(jnp.bfloat16)
    acc = jnp.take(acc, dy, axis=0) + exchange(jnp.take(sent, 1 - dy, axis=0), "dy", 2, 1).astype(
        jnp.float32
    )
    acc = with_layout_constraint(acc.astype(jnp.bfloat16), Layout(major_to_minor=(0, 1)))
    return acc.T


def per_device(gate_pre, up_pre, grad_out, codes, scales):
    weight = decode(codes, scales)
    gate_value = gate_pre.astype(jnp.float32)
    up_value = up_pre.astype(jnp.float32)
    sigmoid_gate = jax.nn.sigmoid(gate_value)
    hidden = (gate_value * sigmoid_gate * up_value).astype(jnp.bfloat16)
    partial_out = jnp.dot(hidden, weight, preferred_element_type=jnp.float32).astype(jnp.bfloat16)
    out = lax.psum_scatter(partial_out, "tz", scatter_dimension=0, tiled=True)
    rows = out.shape[0] // 2
    ty = lax.axis_index("ty")
    out = lax.dynamic_slice_in_dim(out, ty * rows, rows, 0).astype(jnp.float32) + exchange(
        lax.dynamic_slice_in_dim(out, (1 - ty) * rows, rows, 0), "ty", 2, 1
    ).astype(jnp.float32)
    out = out.astype(jnp.bfloat16)
    cotangent = lax.all_gather(grad_out, "ty", axis=0, tiled=True)
    cotangent = lax.all_gather(cotangent, "tz", axis=0, tiled=True)
    grad_hidden = lax.dot_general(
        cotangent, weight, (((1,), (1,)), ((), ())), preferred_element_type=jnp.float32
    )
    grad_weight = weight_gradient(hidden, cotangent)
    grad_gate = (
        grad_hidden * up_value * sigmoid_gate * (1.0 + gate_value * (1.0 - sigmoid_gate))
    ).astype(jnp.bfloat16)
    grad_up = (grad_hidden * gate_value * sigmoid_gate).astype(jnp.bfloat16)
    return (out, grad_gate, grad_up, grad_weight)


def split_mesh(mesh):
    n_dp, n_tensor = (mesh.shape["dp"], mesh.shape["tensor"])
    devices = mesh.devices.reshape(2, n_dp // 4, 2, n_tensor // 2, 2)
    return Mesh(devices, DP + TP)


def solution(mesh):
    fine = split_mesh(mesh)
    in_specs = (P(DP, TP), P(DP, TP), P(DP + TP, None), P(TP, None), P(TP, None))
    out_specs = (P(DP + TP, None), P(DP, TP), P(DP, TP), P(TP, DP))
    return jax.shard_map(
        per_device, mesh=fine, in_specs=in_specs, out_specs=out_specs, check_vma=False
    )
```

profile of v0, /device:TPU:1, one launch (start us, length us, event | category | flops | bytes accessed | tf_op | source)
XLA Modules:
  0.0 170.8 jit_solution(15946947193299180030)
XLA Ops:
  7.2 12.1 %all_gather.6 = bf16[64,4096]{1,0:T(8,128)(2,1)} all-gather(bf16[32,4096]{1,0:T(8,128)(2,1)} %param.11), channel_id=1, replica_groups=mesh['dy'=2,'dx'=4,'dc'=2,'tz'=8,'ty'=2] {'ty'}, dimensions={0}, use_global_device_ids=true | all-gather | bytes 786432 | tf_op jit(solution)/shard_map/all_gather | solution.py:64
  19.5 1.3 copy.17
  20.8 1.3 copy.16
  22.0 0.1 exponential_convert_fusion
  22.2 3.7 %bitcast_multiply_fusion = bf16[896,4096]{1,0:T(8,128)(2,1)S(1)} fusion(bf16[896,4096]{1,0:T(8,128)(2,1)} %param.12, bf16[28,4096]{1,0:T(8,128)(2,1)S(1)} %exponential_convert_fusion), kind=kLoop, calls=%fused_computation | loop fusion | flops 3670016 | bytes 14909440 | tf_op jit(solution)/shard_map/mul | solution.py:13
  25.8 2.9 %copy-done.1 = bf16[896,4096]{1,0:T(8,128)(2,1)} copy-done((bf16[896,4096]{1,0:T(8,128)(2,1)}, bf16[896,4096]{1,0:T(8,128)(2,1)S(1)}, u32[]{:S(2)}) %copy-start.1) | copy-done | bytes 7340056
  28.8 8.1 %convolution_convert_fusion.1 = bf16[512,4096]{1,0:T(8,128)(2,1)} fusion(bf16[896,4096]{1,0:T(8,128)(2,1)S(1)} %bitcast_multiply_fusion, bf16[512,896]{0,1:T(8,128)(2,1)} %copy.17, bf16[512,896]{0,1:T(8,128)(2,1)} %copy.16), kind=kOutput, calls=%fused_computation.3 | convolution fusion | flops 3763863552 | bytes 13369344 | tf_op jit(solution)/shard_map/dot_general | solution.py:56
  36.9 39.5 %all-gather.2.cloned.1.call-done = bf16[512,4096]{1,0:T(8,128)(2,1)} async-done(((bf16[64,4096]{1,0:T(8,128)(2,1)}), bf16[512,4096]{1,0:T(8,128)(2,1)}) %all-gather.2.cloned.1.call-update) | async-done | bytes 4194320 | tf_op jit(solution)/shard_map/all_gather | solution.py:65
  76.5 7.2 %convolution_convert_fusion = bf16[896,4096]{0,1:T(8,128)(2,1)S(1)} fusion(bf16[512,4096]{1,0:T(8,128)(2,1)} %all-gather.2.cloned.1.call-done, bf16[512,896]{0,1:T(8,128)(2,1)S(1)} %copy-done.5, bf16[512,896]{0,1:T(8,128)(2,1)S(1)} %copy-done.7), kind=kOutput, calls=%fused_computation.2 | convolution fusion | flops 3765436416 | bytes 13369344 | tf_op jit(solution)/shard_map/dot_general | solution.py:25
  83.7 3.0 %copy-done.2 = bf16[896,4096]{0,1:T(8,128)(2,1)} copy-done((bf16[896,4096]{0,1:T(8,128)(2,1)}, bf16[896,4096]{0,1:T(8,128)(2,1)S(1)}, u32[]{:S(2)}) %copy-start.2) | copy-done | bytes 7340056
  86.7 2.3 %fusion = bf16[2,4,256,896]{3,2,1,0:T(8,128)(2,1)} fusion(bf16[2,4,2,256,896]{4,3,2,1,0:T(8,128)(2,1)S(1)} %bitcast.52, s32[]{:T(128)S(6)} %select_n.90, pred[]{:T(512)S(6)} %and.53), kind=kLoop, calls=%fused_computation.5 | loop fusion | flops 1835008 | bytes 7340037 | tf_op jit(solution)/shard_map/jit(_take)/select_n | solution.py:32
  89.0 0.8 collective-permute-start.1
  89.8 6.4 %collective-permute-done.1 = bf16[2,4,256,896]{3,2,1,0:T(8,128)(2,1)} collective-permute-done((bf16[2,4,256,896]{3,2,1,0:T(8,128)(2,1)}, bf16[2,4,256,896]{3,2,1,0:T(8,128)(2,1)}, u32[]{:S(2)}, u32[]{:S(2)}) %collective-permute-start.1) | collective-permute-done | bytes 3670048 | tf_op jit(solution)/shard_map/ppermute | solution.py:19
  96.2 4.4 %convert_add_fusion = f32[2,4,256,896]{3,2,1,0:T(8,128)S(1)} fusion(bf16[2,4,256,896]{3,2,1,0:T(8,128)(2,1)} %collective-permute-done.1, bf16[2,4,2,256,896]{4,3,2,1,0:T(8,128)(2,1)} %bitcast.53, s32[]{:T(128)S(6)} %select_n.88, pred[]{:T(512)S(6)} %and.52), kind=kLoop, calls=%fused_computation.1 | loop fusion | flops 7340032 | bytes 14680069 | tf_op jit(solution)/shard_map/add | solution.py:33
  100.6 1.6 select_bitcast_fusion.2
  102.2 2.4 %collective-permute-start.4 = (bf16[2,256,896]{2,1,0:T(8,128)(2,1)}, bf16[2,256,896]{2,1,0:T(8,128)(2,1)}, u32[]{:S(2)}, u32[]{:S(2)}) collective-permute-start(bf16[2,256,896]{2,1,0:T(8,128)(2,1)} %get-tuple-element.70), channel_id=1, source_target_pairs={{0,96},{32,0},{64,32},{96,64},{1,97},{33,1},{65,33},{97,65},{2,98}... | collective-permute-start | bytes 2752520 | tf_op jit(solution)/shard_map/ppermute | solution.py:19
  104.6 0.6 collective-permute-start.3
  105.2 0.6 collective-permute-start.2
  105.8 5.9 %fusion.11 = (bf16[512,896]{0,1:T(8,128)(2,1)}, bf16[512,896]{0,1:T(8,128)(2,1)}) fusion(bf16[512,896]{0,1:T(8,128)(2,1)S(1)} %copy-done.8, bf16[512,896]{0,1:T(8,128)(2,1)S(1)} %copy-done.6, bf16[896,4096]{1,0:T(8,128)(2,1)S(1)} %bitcast.51, bf16[512,4096]{1,0:T(8,128)(2,1)S(1)} %copy-done.12), kind=kOutput, calls=%fused_computation.23 | convolution fusion | flops 3764977664 | bytes 15204352 | tf_op jit(solution)/shard_map/dot_general | solution.py:66
  111.6 2.3 %copy.22 = bf16[512,896]{1,0:T(8,128)(2,1)} copy(bf16[512,896]{0,1:T(8,128)(2,1)} %get-tuple-element.73) | data formatting | bytes 1835008
  114.0 1.3 copy.23
  115.2 17.8 %reduce-scatter.2.cloned.1.call-done = bf16[64,4096]{1,0:T(8,128)(2,1)} async-done(((bf16[512,4096]{1,0:T(8,128)(2,1)}), bf16[64,4096]{1,0:T(8,128)(2,1)}) %reduce-scatter.2.cloned.1.call-update) | async-done | bytes 524304 | tf_op jit(solution)/shard_map/reduce_scatter | solution.py:57
  133.0 1.0 constant_dynamic-slice_fusion
  134.0 2.8 %collective-permute-start = (bf16[32,4096]{1,0:T(8,128)(2,1)S(1)}, bf16[32,4096]{1,0:T(8,128)(2,1)S(1)}, u32[]{:S(2)}, u32[]{:S(2)}) collective-permute-start(bf16[32,4096]{1,0:T(8,128)(2,1)S(1)} %constant_dynamic-slice_fusion), channel_id=1, source_target_pairs={{0,1},{1,0},{2,3},{3,2},{4,5},{5,4},{6,7},{7,6},{8,9},{9,8},{10,11... | collective-permute-start | bytes 786440 | tf_op jit(solution)/shard_map/ppermute | solution.py:19
  136.9 11.5 %collective-permute-done.2 = bf16[2,256,896]{2,1,0:T(8,128)(2,1)} collective-permute-done((bf16[2,256,896]{2,1,0:T(8,128)(2,1)}, bf16[2,256,896]{2,1,0:T(8,128)(2,1)}, u32[]{:S(2)}, u32[]{:S(2)}) %collective-permute-start.2) | collective-permute-done | bytes 917536 | tf_op jit(solution)/shard_map/ppermute | solution.py:19
  148.4 2.8 %fusion.13 = f32[2,256,896]{2,1,0:T(8,128)S(1)} fusion(s32[]{:T(128)S(6)} %select_n.60, bf16[2,256,896]{2,1,0:T(8,128)(2,1)} %collective-permute-done.4, bf16[2,256,896]{2,1,0:T(8,128)(2,1)} %collective-permute-done.3, bf16[2,256,896]{2,1,0:T(8,128)(2,1)} %collective-permute-done.2, pred[]{:T(512)S(6)} %and.50, f32[2,4,256,896]{3,2,1,0:T(8,128)} %copy-done), kind=kLoop, calls=%fused_computation.26 | loop fusion | flops 3211264 | bytes 6422533 | tf_op jit(solution)/shard_map/add | solution.py:40
  151.1 0.1 fusion.17
  151.2 1.3 collective-permute-start.5
  152.5 0.8 add_convert_fusion
  153.3 9.6 %collective-permute-done.5 = bf16[256,896]{1,0:T(8,128)(2,1)S(1)} collective-permute-done((bf16[256,896]{1,0:T(8,128)(2,1)S(1)}, bf16[256,896]{1,0:T(8,128)(2,1)S(1)}, u32[]{:S(2)}, u32[]{:S(2)}) %collective-permute-start.5) | collective-permute-done | bytes 458784 | tf_op jit(solution)/shard_map/ppermute | solution.py:19
  162.9 0.1 fusion.15
  163.0 1.0 copy.24
  (36 shorter events, 0.2 us)
Async XLA Ops:
  7.2 12.3 %copy-start.3 = (bf16[512,896]{1,0:T(8,128)(2,1)S(1)}, bf16[512,896]{1,0:T(8,128)(2,1)}, u32[]{:S(2)}) copy-start(bf16[512,896]{1,0:T(8,128)(2,1)} %param.10) | copy-start | bytes 2752516
  7.2 13.6 %copy-start.4 = (bf16[512,896]{1,0:T(8,128)(2,1)S(1)}, bf16[512,896]{1,0:T(8,128)(2,1)}, u32[]{:S(2)}) copy-start(bf16[512,896]{1,0:T(8,128)(2,1)} %param.9) | copy-start | bytes 2752516
  7.2 69.3 %all-gather.2.cloned.1.call-start = ((), (), s32[]{:S(2)}) async-start(), calls=%async_computation.2 | async-start | bytes 4718592 | tf_op jit(solution)/shard_map/all_gather | solution.py:65
  19.4 2.6 %copy-start.10 = (s32[28,4096]{1,0:T(8,128)S(1)}, s32[28,4096]{1,0:T(8,128)}, u32[]{:S(2)}) copy-start(s32[28,4096]{1,0:T(8,128)} %param.13) | copy-start | bytes 1376260
  19.4 113.6 %reduce-scatter.2.cloned.1.call-start = ((), (), s32[]{:S(2)}) async-start(), calls=%async_computation.1 | async-start | bytes 4718592 | tf_op jit(solution)/shard_map/reduce_scatter | solution.py:57
  25.8 2.9 %copy-start.1 = (bf16[896,4096]{1,0:T(8,128)(2,1)}, bf16[896,4096]{1,0:T(8,128)(2,1)S(1)}, u32[]{:S(2)}) copy-start(bf16[896,4096]{1,0:T(8,128)(2,1)S(1)} %bitcast_multiply_fusion) | copy-start | bytes 22020100
  36.9 39.6 %copy-start.5 = (bf16[512,896]{0,1:T(8,128)(2,1)S(1)}, bf16[512,896]{0,1:T(8,128)(2,1)}, u32[]{:S(2)}) copy-start(bf16[512,896]{0,1:T(8,128)(2,1)} %copy.17) | copy-start | bytes 2752516
  36.9 39.6 %copy-start.7 = (bf16[512,896]{0,1:T(8,128)(2,1)S(1)}, bf16[512,896]{0,1:T(8,128)(2,1)}, u32[]{:S(2)}) copy-start(bf16[512,896]{0,1:T(8,128)(2,1)} %copy.16) | copy-start | bytes 2752516
  83.7 3.0 %copy-start.2 = (bf16[896,4096]{0,1:T(8,128)(2,1)}, bf16[896,4096]{0,1:T(8,128)(2,1)S(1)}, u32[]{:S(2)}) copy-start(bf16[896,4096]{0,1:T(8,128)(2,1)S(1)} %convolution_convert_fusion) | copy-start | bytes 22020100
  86.7 19.1 %slice-start = ((s8[7340032]{0:T(1024)(128)(4,1)}), s8[3145728]{0:T(1024)(128)(4,1)S(1)}, s32[]{:S(2)}) async-start(s8[7340032]{0:T(1024)(128)(4,1)} %bitcast.50), calls=%async_computation.3 | async-start | bytes 6291456
  89.0 7.2 %collective-permute-start.1 = (bf16[2,4,256,896]{3,2,1,0:T(8,128)(2,1)}, bf16[2,4,256,896]{3,2,1,0:T(8,128)(2,1)}, u32[]{:S(2)}, u32[]{:S(2)}) collective-permute-start(bf16[2,4,256,896]{3,2,1,0:T(8,128)(2,1)} %fusion), channel_id=1, source_target_pairs={{0,16},{16,0},{1,17},{17,1},{2,18},{18,2},{3,19},{19,3},{4,20},{20... | collective-permute-start | bytes 11010056 | tf_op jit(solution)/shard_map/ppermute | solution.py:19
  89.8 15.9 %slice-start.1 = ((s8[7340032]{0:T(1024)(128)(4,1)}), s8[4194304]{0:T(1024)(128)(4,1)S(1)}, s32[]{:S(2)}) async-start(s8[7340032]{0:T(1024)(128)(4,1)} %bitcast.50), calls=%async_computation.4 | async-start | bytes 8388608
  96.2 9.6 %copy-start.12 = (bf16[512,4096]{1,0:T(8,128)(2,1)S(1)}, bf16[512,4096]{1,0:T(8,128)(2,1)}, u32[]{:S(2)}) copy-start(bf16[512,4096]{1,0:T(8,128)(2,1)} %all-gather.2.cloned.1.call-done) | copy-start | bytes 12582916
  100.6 11.1 %copy-start = (f32[2,4,256,896]{3,2,1,0:T(8,128)}, f32[2,4,256,896]{3,2,1,0:T(8,128)S(1)}, u32[]{:S(2)}) copy-start(f32[2,4,256,896]{3,2,1,0:T(8,128)S(1)} %convert_add_fusion) | copy-start | bytes 22020100
  100.6 5.2 %copy-start.6 = (bf16[512,896]{0,1:T(8,128)(2,1)S(1)}, bf16[512,896]{0,1:T(8,128)(2,1)}, u32[]{:S(2)}) copy-start(bf16[512,896]{0,1:T(8,128)(2,1)} %copy.17) | copy-start | bytes 2752516
  100.6 5.2 %copy-start.8 = (bf16[512,896]{0,1:T(8,128)(2,1)S(1)}, bf16[512,896]{0,1:T(8,128)(2,1)}, u32[]{:S(2)}) copy-start(bf16[512,896]{0,1:T(8,128)(2,1)} %copy.16) | copy-start | bytes 2752516
  102.2 34.6 %collective-permute-start.4 = (bf16[2,256,896]{2,1,0:T(8,128)(2,1)}, bf16[2,256,896]{2,1,0:T(8,128)(2,1)}, u32[]{:S(2)}, u32[]{:S(2)}) collective-permute-start(bf16[2,256,896]{2,1,0:T(8,128)(2,1)} %get-tuple-element.70), channel_id=1, source_target_pairs={{0,96},{32,0},{64,32},{96,64},{1,97},{33,1},{65,33},{97,65},{2,98}... | collective-permute-start | bytes 2752520 | tf_op jit(solution)/shard_map/ppermute | solution.py:19
  104.6 32.2 %collective-permute-start.3 = (bf16[2,256,896]{2,1,0:T(8,128)(2,1)}, bf16[2,256,896]{2,1,0:T(8,128)(2,1)}, u32[]{:S(2)}, u32[]{:S(2)}) collective-permute-start(bf16[2,256,896]{2,1,0:T(8,128)(2,1)} %get-tuple-element.71), channel_id=1, source_target_pairs={{0,64},{32,96},{64,0},{96,32},{1,65},{33,97},{65,1},{97,33},{2,66}... | collective-permute-start | bytes 2752520 | tf_op jit(solution)/shard_map/ppermute | solution.py:19
  105.2 43.2 %collective-permute-start.2 = (bf16[2,256,896]{2,1,0:T(8,128)(2,1)}, bf16[2,256,896]{2,1,0:T(8,128)(2,1)}, u32[]{:S(2)}, u32[]{:S(2)}) collective-permute-start(bf16[2,256,896]{2,1,0:T(8,128)(2,1)} %get-tuple-element.69), channel_id=1, source_target_pairs={{0,32},{32,64},{64,96},{96,0},{1,33},{33,65},{65,97},{97,1},{2,34}... | collective-permute-start | bytes 2752520 | tf_op jit(solution)/shard_map/ppermute | solution.py:19
  111.6 2.3 %copy-start.9 = (bf16[512,896]{0,1:T(8,128)(2,1)S(1)}, bf16[512,896]{0,1:T(8,128)(2,1)}, u32[]{:S(2)}) copy-start(bf16[512,896]{0,1:T(8,128)(2,1)} %get-tuple-element.72) | copy-start | bytes 2752516
  134.0 18.5 %copy-start.11 = (bf16[64,4096]{1,0:T(8,128)(2,1)S(1)}, bf16[64,4096]{1,0:T(8,128)(2,1)}, u32[]{:S(2)}) copy-start(bf16[64,4096]{1,0:T(8,128)(2,1)} %reduce-scatter.2.cloned.1.call-done) | copy-start | bytes 1572868
  134.0 18.5 %collective-permute-start = (bf16[32,4096]{1,0:T(8,128)(2,1)S(1)}, bf16[32,4096]{1,0:T(8,128)(2,1)S(1)}, u32[]{:S(2)}, u32[]{:S(2)}) collective-permute-start(bf16[32,4096]{1,0:T(8,128)(2,1)S(1)} %constant_dynamic-slice_fusion), channel_id=1, source_target_pairs={{0,1},{1,0},{2,3},{3,2},{4,5},{5,4},{6,7},{7,6},{8,9},{9,8},{10,11... | collective-permute-start | bytes 786440 | tf_op jit(solution)/shard_map/ppermute | solution.py:19
  151.2 11.7 %collective-permute-start.5 = (bf16[256,896]{1,0:T(8,128)(2,1)S(1)}, bf16[256,896]{1,0:T(8,128)(2,1)S(1)}, u32[]{:S(2)}, u32[]{:S(2)}) collective-permute-start(bf16[256,896]{1,0:T(8,128)(2,1)S(1)} %fusion.17), channel_id=1, source_target_pairs={{0,128},{128,0},{1,129},{129,1},{2,130},{130,2},{3,131},{131,3},{4... | collective-permute-start | bytes 1376264 | tf_op jit(solution)/shard_map/ppermute | solution.py:19
Sparse Core Ops, SparseCore 0:
  19.5 56.8 all-gather.1
  79.0 54.0 reduce-scatter.1
where the time goes:
time: 171 us
  waiting for transfers between devices  84.9 us (50%)
  matrix products  21.2 us (12%)
  other arithmetic  15.8 us (9%)
  between operations  14.2 us (8%)
  local copies, waits for them, and re-layouts  14.1 us (8%)
  blocking collectives  12.1 us (7%)
  starting transfers between devices  8.59 us (5%)
    all_gather x1, waiting for transfers between devices, per_device(): cotangent = lax.all_gather(cotangent, 'tz', axis=0, tiled=True)  39.5 us
    ppermute x6, waiting for transfers between devices, exchange(): return lax.ppermute(value, axis, perm)  27.5 us
    reduce_scatter x1, waiting for transfers between devices, per_device(): out = lax.psum_scatter(partial_out, 'tz', scatter_dimension=0, tiled=True)  17.8 us
    unnamed x35, local copies, waits for them, and re-layouts  13.1 us
    all_gather x1, blocking collectives, per_device(): cotangent = lax.all_gather(grad_out, 'ty', axis=0, tiled=True)  12.1 us
    ppermute x6, starting transfers between devices, exchange(): return lax.ppermute(value, axis, perm)  8.51 us
    dot_general x1, matrix products, per_device(): jnp.dot(hidden, weight, preferred_element_type=jnp.float32)  8.1 us
    dot_general x1, matrix products, weight_gradient(): lax.dot_general(cotangent, hidden, (((0,), (0,)), ((), ())), preferred_el...  7.19 us
  transfers between devices with their start and end apart: 8, of which 5 were waited for; matrix products, arithmetic and copies ran while one was open for 26% of the time, Pallas kernels for 0%

commit v1 on v0

--- a/solution.py
+++ b/solution.py
@@ -61,7 +61,9 @@
         lax.dynamic_slice_in_dim(out, (1 - ty) * rows, rows, 0), "ty", 2, 1
     ).astype(jnp.float32)
     out = out.astype(jnp.bfloat16)
-    cotangent = lax.all_gather(grad_out, "ty", axis=0, tiled=True)
+    cotangent = jnp.concatenate(
+        lax.all_to_all(jnp.stack([grad_out] * lax.axis_size("ty")), "ty", 0, 0), axis=0
+    )
     cotangent = lax.all_gather(cotangent, "tz", axis=0, tiled=True)
     grad_hidden = lax.dot_general(
         cotangent, weight, (((1,), (1,)), ((), ())), preferred_element_type=jnp.float32

time: 171 us -> 176 us (1.029)
  waiting for transfers between devices: 84.9 us -> 90.7 us
  local copies, waits for them, and re-layouts: 14.1 us -> 10.9 us
    all_to_all x0 -> x1, blocking collectives: none -> 13.1 us  [per_device(): lax.all_to_all(jnp.stack([grad_out] * lax.axis_size('ty')), 'ty', 0, 0)]
    all_gather x1 -> x0, blocking collectives: 12.1 us -> none  [per_device(): cotangent = lax.all_gather(grad_out, 'ty', axis=0, tiled=True)]
    unnamed x35 -> x25, local copies, waits for them, and re-layouts: 13.1 us -> 9.98 us
    ppermute x6, waiting for transfers between devices: 27.5 us -> 30.5 us  [exchange(): return lax.ppermute(value, axis, perm)]
    all_gather x1, waiting for transfers between devices: 39.5 us -> 42.2 us  [per_device(): cotangent = lax.all_gather(cotangent, 'tz', axis=0, tiled=True)]
  transfers between devices with their start and end apart: 8 -> 8, of which waited for: 5 -> 5; matrix products, arithmetic and copies ran while one was open for 26% -> 22% of each run, Pallas kernels for 0% -> 0%
where the time goes in v1:
time: 176 us
  waiting for transfers between devices  90.7 us (52%)
  matrix products  21.3 us (12%)
  other arithmetic  16.9 us (10%)
  between operations  14.2 us (8%)
  blocking collectives  13.1 us (7%)
  local copies, waits for them, and re-layouts  10.9 us (6%)
  starting transfers between devices  8.59 us (5%)
    all_gather x1, waiting for transfers between devices, per_device(): cotangent = lax.all_gather(cotangent, 'tz', axis=0, tiled=True)  42.2 us
    ppermute x6, waiting for transfers between devices, exchange(): return lax.ppermute(value, axis, perm)  30.5 us
    reduce_scatter x1, waiting for transfers between devices, per_device(): out = lax.psum_scatter(partial_out, 'tz', scatter_dimension=0, tiled=True)  18 us
    all_to_all x1, blocking collectives, per_device(): lax.all_to_all(jnp.stack([grad_out] * lax.axis_size('ty')), 'ty', 0, 0)  13.1 us
    unnamed x25, local copies, waits for them, and re-layouts  9.98 us
    ppermute x6, starting transfers between devices, exchange(): return lax.ppermute(value, axis, perm)  8.51 us
    dot_general x1, matrix products, per_device(): jnp.dot(hidden, weight, preferred_element_type=jnp.float32)  7.76 us
    dot_general x1, matrix products, weight_gradient(): lax.dot_general(cotangent, hidden, (((0,), (0,)), ((), ())), preferred_el...  7.21 us
  transfers between devices with their start and end apart: 8, of which 5 were waited for; matrix products, arithmetic and copies ran while one was open for 22% of the time, Pallas kernels for 0%

profile of v1, /device:TPU:1, one launch (start us, length us, event | category | flops | bytes accessed | tf_op | source)
XLA Modules:
  0.0 175.6 jit_solution(11734605136930083433)
XLA Ops:
  7.2 0.0 all-gather.2.cloned.1.call-start
  7.2 1.1 pad_maximum_fusion
  8.4 13.1 %all_to_all.5 = bf16[2,32,4096]{2,1,0:T(8,128)(2,1)} all-to-all(bf16[2,32,4096]{2,1,0:T(8,128)(2,1)S(1)} %pad_maximum_fusion), channel_id=1, replica_groups=mesh['dy'=2,'dx'=4,'dc'=2,'tz'=8,'ty'=2] {'ty'}, dimensions={0} | all-to-all | bytes 1048576 | tf_op jit(solution)/shard_map/all_to_all | solution.py:65
  21.4 0.0 reduce-scatter.2.cloned.1.call-start
  21.5 0.1 exponential_convert_fusion
  21.6 3.7 %bitcast_multiply_fusion = bf16[896,4096]{1,0:T(8,128)(2,1)S(1)} fusion(bf16[896,4096]{1,0:T(8,128)(2,1)} %param.12, bf16[28,4096]{1,0:T(8,128)(2,1)S(1)} %exponential_convert_fusion), kind=kLoop, calls=%fused_computation | loop fusion | flops 3670016 | bytes 14909440 | tf_op jit(solution)/shard_map/mul | solution.py:13
  25.3 2.9 %copy-done.1 = bf16[896,4096]{1,0:T(8,128)(2,1)} copy-done((bf16[896,4096]{1,0:T(8,128)(2,1)}, bf16[896,4096]{1,0:T(8,128)(2,1)S(1)}, u32[]{:S(2)}) %copy-start.1) | copy-done | bytes 7340056
  28.2 7.8 %convolution_convert_fusion.1 = bf16[512,4096]{1,0:T(8,128)(2,1)} fusion(bf16[896,4096]{1,0:T(8,128)(2,1)S(1)} %bitcast_multiply_fusion, bf16[512,896]{1,0:T(8,128)(2,1)} %param.10, bf16[512,896]{1,0:T(8,128)(2,1)} %param.9), kind=kOutput, calls=%fused_computation.3 | convolution fusion | flops 3763863552 | bytes 13369344 | tf_op jit(solution)/shard_map/dot_general | solution.py:56
  36.0 42.2 %all-gather.2.cloned.1.call-done = bf16[512,4096]{1,0:T(8,128)(2,1)} async-done(((bf16[64,4096]{1,0:T(8,128)(2,1)}), bf16[512,4096]{1,0:T(8,128)(2,1)}) %all-gather.2.cloned.1.call-update) | async-done | bytes 4194320 | tf_op jit(solution)/shard_map/all_gather | solution.py:67
  78.2 7.2 %convolution_convert_fusion = bf16[4096,896]{1,0:T(8,128)(2,1)S(1)} fusion(bf16[512,4096]{1,0:T(8,128)(2,1)} %all-gather.2.cloned.1.call-done, bf16[512,896]{1,0:T(8,128)(2,1)S(1)} %copy-done.6, bf16[512,896]{1,0:T(8,128)(2,1)S(1)} %copy-done.8), kind=kOutput, calls=%fused_computation.2 | convolution fusion | flops 3765436416 | bytes 13369344 | tf_op jit(solution)/shard_map/dot_general | solution.py:25
  85.5 3.0 %copy-done.2 = bf16[4096,896]{1,0:T(8,128)(2,1)} copy-done((bf16[4096,896]{1,0:T(8,128)(2,1)}, bf16[4096,896]{1,0:T(8,128)(2,1)S(1)}, u32[]{:S(2)}) %copy-start.2) | copy-done | bytes 7340056
  88.5 2.3 %fusion = bf16[2,4,256,896]{3,2,1,0:T(8,128)(2,1)} fusion(bf16[2,4,2,256,896]{4,3,2,1,0:T(8,128)(2,1)S(1)} %bitcast.49, s32[]{:T(128)S(6)} %select_n.90, pred[]{:T(512)S(6)} %and.53), kind=kLoop, calls=%fused_computation.5 | loop fusion | flops 1835008 | bytes 7340037 | tf_op jit(solution)/shard_map/jit(_take)/select_n | solution.py:32
  90.8 0.8 collective-permute-start.1
  91.6 6.4 %collective-permute-done.1 = bf16[2,4,256,896]{3,2,1,0:T(8,128)(2,1)} collective-permute-done((bf16[2,4,256,896]{3,2,1,0:T(8,128)(2,1)}, bf16[2,4,256,896]{3,2,1,0:T(8,128)(2,1)}, u32[]{:S(2)}, u32[]{:S(2)}) %collective-permute-start.1) | collective-permute-done | bytes 3670048 | tf_op jit(solution)/shard_map/ppermute | solution.py:19
  98.0 4.3 %convert_add_fusion = f32[2,4,256,896]{3,2,1,0:T(8,128)S(1)} fusion(bf16[2,4,256,896]{3,2,1,0:T(8,128)(2,1)} %collective-permute-done.1, bf16[2,4,2,256,896]{4,3,2,1,0:T(8,128)(2,1)} %bitcast.50, s32[]{:T(128)S(6)} %select_n.88, pred[]{:T(512)S(6)} %and.52), kind=kLoop, calls=%fused_computation.1 | loop fusion | flops 7340032 | bytes 14680069 | tf_op jit(solution)/shard_map/add | solution.py:33
  102.3 3.0 %copy-done = f32[2,4,256,896]{3,2,1,0:T(8,128)} copy-done((f32[2,4,256,896]{3,2,1,0:T(8,128)}, f32[2,4,256,896]{3,2,1,0:T(8,128)S(1)}, u32[]{:S(2)}) %copy-start) | copy-done | bytes 7340056
  105.4 1.6 select_bitcast_fusion.2
  107.0 2.4 %collective-permute-start.4 = (bf16[2,256,896]{2,1,0:T(8,128)(2,1)}, bf16[2,256,896]{2,1,0:T(8,128)(2,1)}, u32[]{:S(2)}, u32[]{:S(2)}) collective-permute-start(bf16[2,256,896]{2,1,0:T(8,128)(2,1)} %get-tuple-element.70), channel_id=1, source_target_pairs={{0,96},{32,0},{64,32},{96,64},{1,97},{33,1},{65,33},{97,65},{2,98}... | collective-permute-start | bytes 2752520 | tf_op jit(solution)/shard_map/ppermute | solution.py:19
  109.4 0.6 collective-permute-start.3
  110.0 0.6 collective-permute-start.2
  110.6 6.3 %fusion.11 = (bf16[512,896]{1,0:T(8,128)(2,1)}, bf16[512,896]{1,0:T(8,128)(2,1)}) fusion(bf16[512,896]{1,0:T(8,128)(2,1)S(1)} %copy-done.9, bf16[512,896]{1,0:T(8,128)(2,1)S(1)} %copy-done.7, bf16[512,4096]{1,0:T(8,128)(2,1)S(1)} %copy-done.5, bf16[896,4096]{1,0:T(8,128)(2,1)S(1)} %bitcast.48), kind=kOutput, calls=%fused_computation.23 | convolution fusion | flops 3764977664 | bytes 15204352 | tf_op jit(solution)/shard_map/dot_general | solution.py:68
  116.9 18.0 %reduce-scatter.2.cloned.1.call-done = bf16[64,4096]{1,0:T(8,128)(2,1)} async-done(((bf16[512,4096]{1,0:T(8,128)(2,1)}), bf16[64,4096]{1,0:T(8,128)(2,1)}) %reduce-scatter.2.cloned.1.call-update) | async-done | bytes 524304 | tf_op jit(solution)/shard_map/reduce_scatter | solution.py:57
  134.8 1.0 constant_dynamic-slice_fusion
  135.8 2.8 %collective-permute-start = (bf16[32,4096]{1,0:T(8,128)(2,1)S(1)}, bf16[32,4096]{1,0:T(8,128)(2,1)S(1)}, u32[]{:S(2)}, u32[]{:S(2)}) collective-permute-start(bf16[32,4096]{1,0:T(8,128)(2,1)S(1)} %constant_dynamic-slice_fusion), channel_id=1, source_target_pairs={{0,1},{1,0},{2,3},{3,2},{4,5},{5,4},{6,7},{7,6},{8,9},{9,8},{10,11... | collective-permute-start | bytes 786440 | tf_op jit(solution)/shard_map/ppermute | solution.py:19
  138.6 14.5 %collective-permute-done.2 = bf16[2,256,896]{2,1,0:T(8,128)(2,1)} collective-permute-done((bf16[2,256,896]{2,1,0:T(8,128)(2,1)}, bf16[2,256,896]{2,1,0:T(8,128)(2,1)}, u32[]{:S(2)}, u32[]{:S(2)}) %collective-permute-start.2) | collective-permute-done | bytes 917536 | tf_op jit(solution)/shard_map/ppermute | solution.py:19
  153.2 2.8 %fusion.13 = f32[2,256,896]{2,1,0:T(8,128)S(1)} fusion(s32[]{:T(128)S(6)} %select_n.60, bf16[2,256,896]{2,1,0:T(8,128)(2,1)} %collective-permute-done.4, bf16[2,256,896]{2,1,0:T(8,128)(2,1)} %collective-permute-done.3, bf16[2,256,896]{2,1,0:T(8,128)(2,1)} %collective-permute-done.2, pred[]{:T(512)S(6)} %and.50, f32[2,4,256,896]{3,2,1,0:T(8,128)} %copy-done), kind=kLoop, calls=%fused_computation.26 | loop fusion | flops 3211264 | bytes 6422533 | tf_op jit(solution)/shard_map/add | solution.py:40
  155.9 0.1 fusion.17
  156.0 1.3 collective-permute-start.5
  157.3 0.8 add_convert_fusion
  158.1 9.6 %collective-permute-done.5 = bf16[256,896]{1,0:T(8,128)(2,1)S(1)} collective-permute-done((bf16[256,896]{1,0:T(8,128)(2,1)S(1)}, bf16[256,896]{1,0:T(8,128)(2,1)S(1)}, u32[]{:S(2)}, u32[]{:S(2)}) %collective-permute-start.5) | collective-permute-done | bytes 458784 | tf_op jit(solution)/shard_map/ppermute | solution.py:19
  167.7 0.1 fusion.15
  167.8 1.0 copy.16
  (27 shorter events, 0.1 us)
Async XLA Ops:
  7.2 14.3 %copy-start.3 = (s32[28,4096]{1,0:T(8,128)S(1)}, s32[28,4096]{1,0:T(8,128)}, u32[]{:S(2)}) copy-start(s32[28,4096]{1,0:T(8,128)} %param.13) | copy-start | bytes 1376260
  7.2 71.1 %all-gather.2.cloned.1.call-start = ((), (), s32[]{:S(2)}) async-start(), calls=%async_computation.3 | async-start | bytes 4718592 | tf_op jit(solution)/shard_map/all_gather | solution.py:67
  21.4 113.4 %reduce-scatter.2.cloned.1.call-start = ((), (), s32[]{:S(2)}) async-start(), calls=%async_computation.2 | async-start | bytes 4718592 | tf_op jit(solution)/shard_map/reduce_scatter | solution.py:57
  25.3 2.9 %copy-start.1 = (bf16[896,4096]{1,0:T(8,128)(2,1)}, bf16[896,4096]{1,0:T(8,128)(2,1)S(1)}, u32[]{:S(2)}) copy-start(bf16[896,4096]{1,0:T(8,128)(2,1)S(1)} %bitcast_multiply_fusion) | copy-start | bytes 22020100
  36.0 42.2 %copy-start.6 = (bf16[512,896]{1,0:T(8,128)(2,1)S(1)}, bf16[512,896]{1,0:T(8,128)(2,1)}, u32[]{:S(2)}) copy-start(bf16[512,896]{1,0:T(8,128)(2,1)} %param.10) | copy-start | bytes 2752516
  36.0 42.2 %copy-start.8 = (bf16[512,896]{1,0:T(8,128)(2,1)S(1)}, bf16[512,896]{1,0:T(8,128)(2,1)}, u32[]{:S(2)}) copy-start(bf16[512,896]{1,0:T(8,128)(2,1)} %param.9) | copy-start | bytes 2752516
  85.5 3.0 %copy-start.2 = (bf16[4096,896]{1,0:T(8,128)(2,1)}, bf16[4096,896]{1,0:T(8,128)(2,1)S(1)}, u32[]{:S(2)}) copy-start(bf16[4096,896]{1,0:T(8,128)(2,1)S(1)} %convolution_convert_fusion) | copy-start | bytes 22020100
  88.5 22.1 %slice-start = ((s8[7340032]{0:T(1024)(128)(4,1)}), s8[3145728]{0:T(1024)(128)(4,1)S(1)}, s32[]{:S(2)}) async-start(s8[7340032]{0:T(1024)(128)(4,1)} %bitcast.47), calls=%async_computation.4 | async-start | bytes 6291456
  90.8 7.2 %collective-permute-start.1 = (bf16[2,4,256,896]{3,2,1,0:T(8,128)(2,1)}, bf16[2,4,256,896]{3,2,1,0:T(8,128)(2,1)}, u32[]{:S(2)}, u32[]{:S(2)}) collective-permute-start(bf16[2,4,256,896]{3,2,1,0:T(8,128)(2,1)} %fusion), channel_id=1, source_target_pairs={{0,16},{16,0},{1,17},{17,1},{2,18},{18,2},{3,19},{19,3},{4,20},{20... | collective-permute-start | bytes 11010056 | tf_op jit(solution)/shard_map/ppermute | solution.py:19
  91.6 18.9 %slice-start.1 = ((s8[7340032]{0:T(1024)(128)(4,1)}), s8[4194304]{0:T(1024)(128)(4,1)S(1)}, s32[]{:S(2)}) async-start(s8[7340032]{0:T(1024)(128)(4,1)} %bitcast.47), calls=%async_computation.5 | async-start | bytes 8388608
  98.0 12.5 %copy-start.9 = (bf16[512,896]{1,0:T(8,128)(2,1)S(1)}, bf16[512,896]{1,0:T(8,128)(2,1)}, u32[]{:S(2)}) copy-start(bf16[512,896]{1,0:T(8,128)(2,1)} %param.9) | copy-start | bytes 2752516
  102.3 3.0 %copy-start = (f32[2,4,256,896]{3,2,1,0:T(8,128)}, f32[2,4,256,896]{3,2,1,0:T(8,128)S(1)}, u32[]{:S(2)}) copy-start(f32[2,4,256,896]{3,2,1,0:T(8,128)S(1)} %convert_add_fusion) | copy-start | bytes 22020100
  105.4 5.2 %copy-start.5 = (bf16[512,4096]{1,0:T(8,128)(2,1)S(1)}, bf16[512,4096]{1,0:T(8,128)(2,1)}, u32[]{:S(2)}) copy-start(bf16[512,4096]{1,0:T(8,128)(2,1)} %all-gather.2.cloned.1.call-done) | copy-start | bytes 12582916
  105.4 5.2 %copy-start.7 = (bf16[512,896]{1,0:T(8,128)(2,1)S(1)}, bf16[512,896]{1,0:T(8,128)(2,1)}, u32[]{:S(2)}) copy-start(bf16[512,896]{1,0:T(8,128)(2,1)} %param.10) | copy-start | bytes 2752516
  107.0 31.6 %collective-permute-start.4 = (bf16[2,256,896]{2,1,0:T(8,128)(2,1)}, bf16[2,256,896]{2,1,0:T(8,128)(2,1)}, u32[]{:S(2)}, u32[]{:S(2)}) collective-permute-start(bf16[2,256,896]{2,1,0:T(8,128)(2,1)} %get-tuple-element.70), channel_id=1, source_target_pairs={{0,96},{32,0},{64,32},{96,64},{1,97},{33,1},{65,33},{97,65},{2,98}... | collective-permute-start | bytes 2752520 | tf_op jit(solution)/shard_map/ppermute | solution.py:19
  109.4 29.2 %collective-permute-start.3 = (bf16[2,256,896]{2,1,0:T(8,128)(2,1)}, bf16[2,256,896]{2,1,0:T(8,128)(2,1)}, u32[]{:S(2)}, u32[]{:S(2)}) collective-permute-start(bf16[2,256,896]{2,1,0:T(8,128)(2,1)} %get-tuple-element.71), channel_id=1, source_target_pairs={{0,64},{32,96},{64,0},{96,32},{1,65},{33,97},{65,1},{97,33},{2,66}... | collective-permute-start | bytes 2752520 | tf_op jit(solution)/shard_map/ppermute | solution.py:19
  110.0 43.2 %collective-permute-start.2 = (bf16[2,256,896]{2,1,0:T(8,128)(2,1)}, bf16[2,256,896]{2,1,0:T(8,128)(2,1)}, u32[]{:S(2)}, u32[]{:S(2)}) collective-permute-start(bf16[2,256,896]{2,1,0:T(8,128)(2,1)} %get-tuple-element.69), channel_id=1, source_target_pairs={{0,32},{32,64},{64,96},{96,0},{1,33},{33,65},{65,97},{97,1},{2,34}... | collective-permute-start | bytes 2752520 | tf_op jit(solution)/shard_map/ppermute | solution.py:19
  135.8 21.5 %copy-start.4 = (bf16[64,4096]{1,0:T(8,128)(2,1)S(1)}, bf16[64,4096]{1,0:T(8,128)(2,1)}, u32[]{:S(2)}) copy-start(bf16[64,4096]{1,0:T(8,128)(2,1)} %reduce-scatter.2.cloned.1.call-done) | copy-start | bytes 1572868
  135.8 21.5 %collective-permute-start = (bf16[32,4096]{1,0:T(8,128)(2,1)S(1)}, bf16[32,4096]{1,0:T(8,128)(2,1)S(1)}, u32[]{:S(2)}, u32[]{:S(2)}) collective-permute-start(bf16[32,4096]{1,0:T(8,128)(2,1)S(1)} %constant_dynamic-slice_fusion), channel_id=1, source_target_pairs={{0,1},{1,0},{2,3},{3,2},{4,5},{5,4},{6,7},{7,6},{8,9},{9,8},{10,11... | collective-permute-start | bytes 786440 | tf_op jit(solution)/shard_map/ppermute | solution.py:19
  156.0 11.7 %collective-permute-start.5 = (bf16[256,896]{1,0:T(8,128)(2,1)S(1)}, bf16[256,896]{1,0:T(8,128)(2,1)S(1)}, u32[]{:S(2)}, u32[]{:S(2)}) collective-permute-start(bf16[256,896]{1,0:T(8,128)(2,1)S(1)} %fusion.17), channel_id=1, source_target_pairs={{0,128},{128,0},{1,129},{129,1},{2,130},{130,2},{3,131},{131,3},{4... | collective-permute-start | bytes 1376264 | tf_op jit(solution)/shard_map/ppermute | solution.py:19
Sparse Core Ops, SparseCore 0:
  21.6 56.6 all-gather.1
  80.8 54.0 reduce-scatter.1
